TPU v7x, 128 devices: a whole 4x4x4 slice. The times are simulated.
128 devices in a mesh: lat: 8 (over y_lo, z), lon: 16 (over x, y_hi, core).
Axes of the slice: x: 4, y: 4 (y_hi: 2, y_lo: 2; y = y_hi * 2 + y_lo), z: 4, core: 2. Of those that a mesh axis runs over, the one named last changes fastest.
Arguments:
- starting_sea_elevation: float32 [256, 2048], P('lat', 'lon'), may hold values from -6 to 6
- zonal_integrated_flux: float32 [256, 2048], P('lat', 'lon'), may hold values from -6 to 6
- meridional_integrated_flux: float32 [256, 2048], P('lat', 'lon'), may hold values from -6 to 6
- ocean_strata_total: int32 [256, 2048], P('lat', 'lon'), may hold values from 0 to 8
- thermal_anomaly: float32 [8, 256, 2048], P(None, 'lat', 'lon'), may hold values from -6 to 6
- zonal_baroclinic_velocity: float32 [8, 256, 2048], P(None, 'lat', 'lon'), may hold values from -3 to 3
- meridional_baroclinic_velocity: float32 [8, 256, 2048], P(None, 'lat', 'lon'), may hold values from -3 to 3
- sent_sender_mesh_index: int32 [128, 128, 1024], P(('lat', 'lon')), may hold values from 0 to 4095
- sent_intersection_extent: float32 [128, 128, 1024], P(('lat', 'lon')), may hold values from 0.2 to 1
- sent_entry_tally: int32 [128, 128], P(('lat', 'lon')), may hold values from 0 to 1024, as said below
- received_atmosphere_mesh_index: int32 [128, 128, 1024], P(('lat', 'lon')), may hold values from 0 to 4095
Outputs:
- height_new: float32 [256, 2048], P('lat', 'lon')
- east_new: float32 [256, 2048], P('lat', 'lon')
- north_new: float32 [256, 2048], P('lat', 'lon')
- temperature_new: float32 [8, 256, 2048], P(None, 'lat', 'lon')
- atmosphere_fields: float32 [4, 524288], P(None, ('lat', 'lon'))
Inputs may be any that keep to these rules, and one draw needn't show every extreme that they name: Slots j >= sent_entry_tally[s, d] are unused. In every draw one owner receives exactly 1024 live slots from every device. `sent_sender_mesh_index`: A cell of the sending device's block, numbered row by row. `received_atmosphere_mesh_index`: an atmosphere cell of the receiving owner. `ocean_strata_total`: 0 is land.
All inputs are finite; a program needn't handle non-finite values.
Results may differ from a plain program's by a relative error of at most 0.00017.
Values sent between devices are 32-bit elements; how exact they have to be, the bound alone decides.
No kernel may reach another device: no remote copies, remote signals or barrier semaphores. Data moves between devices by JAX's collectives and lax.ppermute only.
A program may use at most 64 MiB of HBM per device.

v0:
```python
import math
import jax
import jax.numpy as jnp
from jax import lax
from jax.sharding import PartitionSpec as P

VERTICAL_STRATA = 8
STEPS = 4
NF = 4
ACELL = 4096
mass_coef = 0.7
slope_coef = 0.7
spin_coef = 0.3
mix_coef = 0.1
carry_coef = 0.1
block_limit = 8192


def with_halo(block, sides, width, periodic):
    for axis, dim in sides:
        count = lax.axis_size(axis)
        forward = [(i, i + 1) for i in range(count - 1)]
        if periodic:
            forward.append((count - 1, 0))
        backward = [(target, source) for source, target in forward]
        low = lax.ppermute(
            lax.slice_in_dim(block, block.shape[dim] - width, None, axis=dim), axis, forward
        )
        high = lax.ppermute(lax.slice_in_dim(block, 0, width, axis=dim), axis, backward)
        block = jnp.concatenate([low, block, high], axis=dim)
    return block


def widen(fields, signs, width):
    rows = fields.shape[1]
    lon_wide = with_halo(fields, (("lon", 2),), width, True)
    both_wide = with_halo(lon_wide, (("lat", 1),), width, False)
    upper = jnp.flip(lon_wide[:, rows - width :, :], axis=(1, 2))
    sectors = lax.axis_size("lon")
    collected = lax.all_gather(upper[None], "lon", axis=0, tiled=True)
    mirrored = lax.dynamic_index_in_dim(
        collected, sectors - 1 - lax.axis_index("lon"), 0, keepdims=False
    )
    folded = mirrored * signs[:, None, None]
    on_top = lax.axis_index("lat") == lax.axis_size("lat") - 1
    top_rim = jnp.where(on_top, folded, both_wide[:, rows + width :, :])
    return jnp.concatenate([both_wide[:, : rows + width, :], top_rim], axis=1)


def pick_cells(surface_grid, indices):
    fields_count, rows, columns = surface_grid.shape
    table = jnp.transpose(surface_grid, (2, 0, 1)).reshape(columns, fields_count * rows)
    total = indices.shape[0]
    size = math.gcd(total, block_limit)
    blocks = indices.reshape(total // size, size)
    column_ids = jnp.arange(columns)
    row_ids = jnp.arange(rows)

    def one_block(block):
        column_hot = (block[:, None] % columns == column_ids[None, :]).astype(jnp.float32)
        row_hot = (block[:, None] // columns == row_ids[None, :]).astype(jnp.float32)
        by_column = jnp.dot(
            column_hot, table, precision=lax.Precision.HIGHEST, preferred_element_type=jnp.float32
        )
        by_column = by_column.reshape(size, fields_count, rows)
        return jnp.sum(by_column * row_hot[:, None, :], axis=2)

    picked = lax.map(one_block, blocks).reshape(total, fields_count)
    return jnp.transpose(picked)


def spread_cells(values, targets, cells):
    fields_count = values.shape[0]
    total = targets.shape[0]
    size = math.gcd(total, block_limit)
    high_count = cells // 128
    value_blocks = jnp.transpose(values.reshape(fields_count, total // size, size), (1, 0, 2))
    target_blocks = targets.reshape(total // size, size)
    low_ids = jnp.arange(128)
    high_ids = jnp.arange(high_count)

    def add_block(carry, pieces):
        value_block, target_block = pieces
        low_hot = (target_block[:, None] % 128 == low_ids[None, :]).astype(jnp.float32)
        high_hot = (target_block[:, None] // 128 == high_ids[None, :]).astype(jnp.float32)
        weighted = (jnp.transpose(value_block)[:, :, None] * high_hot[:, None, :]).reshape(
            size, fields_count * high_count
        )
        term = lax.dot_general(
            weighted,
            low_hot,
            (((0,), (0,)), ((), ())),
            precision=lax.Precision.HIGHEST,
            preferred_element_type=jnp.float32,
        )
        return (carry + term, None)

    start = jnp.zeros((fields_count * high_count, 128), jnp.float32)
    summed, _ = lax.scan(add_block, start, (value_blocks, target_blocks))
    return summed.reshape(fields_count, cells)


def local(
    starting_sea_elevation,
    zonal_integrated_flux,
    meridional_integrated_flux,
    ocean_strata_total,
    thermal_anomaly,
    zonal_baroclinic_velocity,
    meridional_baroclinic_velocity,
    sent_sender_mesh_index,
    sent_intersection_extent,
    sent_entry_tally,
    received_atmosphere_mesh_index,
):
    band_rows = starting_sea_elevation.shape[0]
    grid_rows = band_rows * lax.axis_size("lat")
    band = lax.axis_index("lat")
    depth = ocean_strata_total.astype(jnp.float32)
    wet = (ocean_strata_total > 0).astype(jnp.float32)
    hnorm = depth / VERTICAL_STRATA
    height = starting_sea_elevation * wet
    east = zonal_integrated_flux * wet
    north = meridional_integrated_flux * wet
    rows = (band * band_rows + jnp.arange(band_rows)).astype(jnp.float32)
    rotation = (-spin_coef * jnp.cos(jnp.pi * (rows + 0.5) / grid_rows))[:, None]
    vector_signs = jnp.array([-1.0, -1.0], jnp.float32)
    scalar_signs = jnp.array([1.0], jnp.float32)
    for step in range(STEPS):
        moved = widen(jnp.stack([east, north]), vector_signs, 1)
        east_e = moved[0, 1:-1, 2:]
        east_w = moved[0, 1:-1, :-2]
        north_n = moved[1, 2:, 1:-1]
        north_s = moved[1, :-2, 1:-1]
        height = wet * (height - mass_coef * (east_e - east_w + (north_n - north_s)))
        height_wide = widen(height[None], scalar_signs, 1)[0]
        height_e = height_wide[1:-1, 2:]
        height_w = height_wide[1:-1, :-2]
        height_n = height_wide[2:, 1:-1]
        height_s = height_wide[:-2, 1:-1]
        east = wet * (east - slope_coef * hnorm * (height_e - height_w) + rotation * north)
        north = wet * (north - slope_coef * hnorm * (height_n - height_s) - rotation * east)
    levels_int = jnp.arange(VERTICAL_STRATA)[:, None, None]
    levels_float = jnp.arange(VERTICAL_STRATA).astype(jnp.float32)[:, None, None]
    submerged_stratum_mask = (levels_int < ocean_strata_total[None]).astype(jnp.float32)
    passive_scalar_values = thermal_anomaly * submerged_stratum_mask
    tracer_signs = jnp.ones((VERTICAL_STRATA + 1,), jnp.float32)
    widened = widen(jnp.concatenate([passive_scalar_values, depth[None]], axis=0), tracer_signs, 1)
    tracer_wide = widened[:VERTICAL_STRATA]
    wet_wide = (levels_float < widened[VERTICAL_STRATA][None]).astype(jnp.float32)
    tracer_e = tracer_wide[:, 1:-1, 2:]
    tracer_w = tracer_wide[:, 1:-1, :-2]
    tracer_n = tracer_wide[:, 2:, 1:-1]
    tracer_s = tracer_wide[:, :-2, 1:-1]
    wet_e = wet_wide[:, 1:-1, 2:]
    wet_w = wet_wide[:, 1:-1, :-2]
    wet_n = wet_wide[:, 2:, 1:-1]
    wet_s = wet_wide[:, :-2, 1:-1]
    mixing = (
        wet_e * (tracer_e - passive_scalar_values)
        + wet_w * (tracer_w - passive_scalar_values)
        + wet_n * (tracer_n - passive_scalar_values)
        + wet_s * (tracer_s - passive_scalar_values)
    )
    speed_east = east[None] + zonal_baroclinic_velocity
    speed_north = north[None] + meridional_baroclinic_velocity
    carried = speed_east * (tracer_e - tracer_w) + speed_north * (tracer_n - tracer_s)
    tracer_new = submerged_stratum_mask * (
        passive_scalar_values + mix_coef * mixing - carry_coef * carried
    )
    surface_grid = jnp.stack([height, speed_east[0], speed_north[0], tracer_new[0]])
    owners = sent_sender_mesh_index.shape[1]
    slots = sent_sender_mesh_index.shape[2]
    picked = pick_cells(surface_grid, sent_sender_mesh_index[0].reshape(-1)).reshape(
        NF, owners, slots
    )
    live = jnp.arange(slots)[None, :] < sent_entry_tally[0][:, None]
    values = jnp.where(live[None], sent_intersection_extent[0][None] * picked, 0.0)
    targets = received_atmosphere_mesh_index[0].reshape(-1)
    block = lax.all_to_all(values, ("lat", "lon"), split_axis=1, concat_axis=1, tiled=True)
    fields_count = block.shape[0]
    atmosphere = spread_cells(block.reshape(fields_count, -1), targets, ACELL)
    return (height, east, north, tracer_new, atmosphere)


def solution(mesh):
    in_specs = (
        P("lat", "lon"),
        P("lat", "lon"),
        P("lat", "lon"),
        P("lat", "lon"),
        P(None, "lat", "lon"),
        P(None, "lat", "lon"),
        P(None, "lat", "lon"),
        P(("lat", "lon"), None, None),
        P(("lat", "lon"), None, None),
        P(("lat", "lon"), None),
        P(("lat", "lon"), None, None),
    )
    out_specs = (
        P("lat", "lon"),
        P("lat", "lon"),
        P("lat", "lon"),
        P(None, "lat", "lon"),
        P(None, ("lat", "lon")),
    )
    return jax.shard_map(local, mesh=mesh, in_specs=in_specs, out_specs=out_specs, check_vma=False)
```

profile of v0, /device:TPU:1, one launch (start us, length us, event | category | flops | bytes accessed | tf_op | source)
XLA Modules:
  0.0 557.0 jit_solution(9308671634009213808)
XLA Ops:
  4.2 2.9 collective-permute-start.1
  14.3 3.5 collective-permute-start.3
  19.4 24.9 %all-gather = f32[32,1,130]{2,1,0:T(1,128)S(1)} all-gather(f32[2,1,130]{2,1,0:T(1,128)S(1)} %slice.507), channel_id=2, replica_groups=mesh['lat'=8,'lon'=16] {'lon'}, dimensions={0}, use_global_device_ids=true | all-gather | bytes 17680 | tf_op jit(solution)/shard_map/all_gather | solution.py:40
  44.5 2.9 collective-permute-start.4
  48.3 3.8 collective-permute-done.5
  52.1 4.3 collective-permute-start.6
  58.0 19.8 %all-gather.1 = f32[16,1,130]{2,1,0:T(1,128)S(1)} all-gather(f32[1,1,130]{2,1,0:T(1,128)S(1)} %slice.508), channel_id=3, replica_groups=mesh['lat'=8,'lon'=16] {'lon'}, dimensions={0}, use_global_device_ids=true | all-gather | bytes 8840 | tf_op jit(solution)/shard_map/all_gather | solution.py:40
  78.5 2.9 collective-permute-start.9
  81.4 4.2 collective-permute-start.34
  86.6 3.4 collective-permute-start.11
  91.5 20.9 %all-gather.2 = f32[32,1,130]{2,1,0:T(1,128)S(1)} all-gather(f32[2,1,130]{2,1,0:T(1,128)S(1)} %slice.509), channel_id=4, replica_groups=mesh['lat'=8,'lon'=16] {'lon'}, dimensions={0}, use_global_device_ids=true | all-gather | bytes 17680 | tf_op jit(solution)/shard_map/all_gather | solution.py:40
  112.7 3.3 collective-permute-start.12
  116.8 3.8 collective-permute-done.13
  120.7 4.3 collective-permute-start.14
  126.5 19.5 %all-gather.3 = f32[16,1,130]{2,1,0:T(1,128)S(1)} all-gather(f32[1,1,130]{2,1,0:T(1,128)S(1)} %slice.510), channel_id=5, replica_groups=mesh['lat'=8,'lon'=16] {'lon'}, dimensions={0}, use_global_device_ids=true | all-gather | bytes 8840 | tf_op jit(solution)/shard_map/all_gather | solution.py:40
  146.6 2.9 collective-permute-start.17
  149.6 19.8 %all-gather.8 = f32[144,1,130]{2,1,0:T(1,128)S(1)} all-gather(f32[9,1,130]{2,1,0:T(1,128)S(1)} %slice.515), channel_id=10, replica_groups=mesh['lat'=8,'lon'=16] {'lon'}, dimensions={0}, use_global_device_ids=true | all-gather | bytes 79560 | tf_op jit(solution)/shard_map/all_gather | solution.py:40
  169.5 6.1 %collective-permute-start.19 = (f32[2,1,130]{2,1,0:T(1,128)S(1)}, f32[2,1,130]{2,1,0:T(1,128)}, u32[]{:S(2)}, u32[]{:S(2)}) collective-permute-start(f32[2,1,130]{2,1,0:T(1,128)S(1)} %get-tuple-element.265), channel_id=1, source_target_pairs={{0,16},{16,32},{32,48},{48,64},{64,80},{80,96},{96,112},{1,17},{17... | collective-permute-start | bytes 3128 | tf_op jit(solution)/shard_map/ppermute | solution.py:26
  177.1 21.3 %all-gather.4 = f32[32,1,130]{2,1,0:T(1,128)S(1)} all-gather(f32[2,1,130]{2,1,0:T(1,128)S(1)} %slice.511), channel_id=6, replica_groups=mesh['lat'=8,'lon'=16] {'lon'}, dimensions={0}, use_global_device_ids=true | all-gather | bytes 17680 | tf_op jit(solution)/shard_map/all_gather | solution.py:40
  202.1 3.7 collective-permute-done.21
  205.8 4.3 collective-permute-start.22
  211.7 20.9 %all-gather.5 = f32[16,1,130]{2,1,0:T(1,128)S(1)} all-gather(f32[1,1,130]{2,1,0:T(1,128)S(1)} %slice.512), channel_id=7, replica_groups=mesh['lat'=8,'lon'=16] {'lon'}, dimensions={0}, use_global_device_ids=true | all-gather | bytes 8840 | tf_op jit(solution)/shard_map/all_gather | solution.py:40
  238.6 6.4 %collective-permute-start.27 = (f32[2,1,130]{2,1,0:T(1,128)S(1)}, f32[2,1,130]{2,1,0:T(1,128)S(1)}, u32[]{:S(2)}, u32[]{:S(2)}) collective-permute-start(f32[2,1,130]{2,1,0:T(1,128)S(1)} %get-tuple-element.263), channel_id=1, source_target_pairs={{0,16},{16,32},{32,48},{48,64},{64,80},{80,96},{96,112},{1,17},{17... | collective-permute-start | bytes 3128 | tf_op jit(solution)/shard_map/ppermute | solution.py:26
  246.5 24.1 %all-gather.6 = f32[32,1,130]{2,1,0:T(1,128)S(1)} all-gather(f32[2,1,130]{2,1,0:T(1,128)S(1)} %slice.513), channel_id=8, replica_groups=mesh['lat'=8,'lon'=16] {'lon'}, dimensions={0}, use_global_device_ids=true | all-gather | bytes 17680 | tf_op jit(solution)/shard_map/all_gather | solution.py:40
  270.8 3.3 collective-permute-start.28
  275.1 3.8 collective-permute-done.29
  280.1 7.1 %collective-permute-start.30 = (f32[1,1,130]{2,1,0:T(1,128)}, f32[1,1,130]{2,1,0:T(1,128)}, u32[]{:S(2)}, u32[]{:S(2)}) collective-permute-start(f32[1,1,130]{2,1,0:T(1,128)} %get-tuple-element.270), channel_id=1, source_target_pairs={{0,16},{16,32},{32,48},{48,64},{64,80},{80,96},{96,112},{1,17},{17... | collective-permute-start | bytes 1568 | tf_op jit(solution)/shard_map/ppermute | solution.py:26
  290.7 19.7 %all-gather.7 = f32[16,1,130]{2,1,0:T(1,128)S(1)} all-gather(f32[1,1,130]{2,1,0:T(1,128)S(1)} %slice.514), channel_id=9, replica_groups=mesh['lat'=8,'lon'=16] {'lon'}, dimensions={0}, use_global_device_ids=true | all-gather | bytes 8840 | tf_op jit(solution)/shard_map/all_gather | solution.py:40
  314.2 62.9 %while.26 = (s32[]{:T(128)}, f32[16,8192,4]{1,2,0:T(4,128)S(1)}, s32[16,8192]{1,0:T(8,128)S(1)}, f32[128,128]{1,0:T(8,128)S(1)}, s32[]{:T(128)}) while((s32[]{:T(128)}, f32[16,8192,4]{1,2,0:T(4,128)S(1)}, s32[16,8192]{1,0:T(8,128)S(1)}, f32[128,128]{1,0:T(8,128)S(1)}, s32[]{:T(128)}) %tuple.96), condition=%wide.region_2.3_spmd.clone, body=%wide.region_0.2_spmd.clone.sunk | while | flops 1614405632 | bytes 2785349 | solution.py:68
  314.3 3.7 multiply_reduce_fusion.2
  318.3 3.7 multiply_reduce_fusion.2
  322.2 3.7 multiply_reduce_fusion.2
  326.1 3.7 multiply_reduce_fusion.2
  330.1 3.7 multiply_reduce_fusion.2
  334.0 3.7 multiply_reduce_fusion.2
  337.9 3.7 multiply_reduce_fusion.2
  341.9 3.7 multiply_reduce_fusion.2
  345.8 3.7 multiply_reduce_fusion.2
  349.7 3.7 multiply_reduce_fusion.2
  353.7 3.7 multiply_reduce_fusion.2
  357.6 3.7 multiply_reduce_fusion.2
  361.5 3.7 multiply_reduce_fusion.2
  365.5 3.7 multiply_reduce_fusion.2
  369.4 3.7 multiply_reduce_fusion.2
  373.3 3.7 multiply_reduce_fusion.2
  382.2 14.8 %all-to-all-start = ((f32[4,128,1024]{2,0,1:T(4,128)}), f32[4,128,1024]{2,0,1:T(4,128)S(1)}, u32[]{:S(2)}, u32[]{:S(2)}) async-start(f32[4,128,1024]{2,0,1:T(4,128)} %copy.26), calls=%async_computation | async-start | bytes 4194304 | tf_op jit(solution)/shard_map/all_to_all | solution.py:180
  398.1 29.0 %all-to-all-done = f32[4,128,1024]{2,0,1:T(4,128)S(1)} async-done(((f32[4,128,1024]{2,0,1:T(4,128)}), f32[4,128,1024]{2,0,1:T(4,128)S(1)}, u32[]{:S(2)}, u32[]{:S(2)}) %all-to-all-start) | async-done | bytes 2097184 | tf_op jit(solution)/shard_map/all_to_all | solution.py:180
  431.5 124.9 %while.27 = (s32[]{:T(128)}, f32[128,128]{1,0:T(8,128)S(1)}, f32[16,4,8192]{2,0,1:T(8,128)S(1)}, s32[16,8192]{1,0:T(8,128)S(1)}, s32[]{:T(128)}, /*index=5*/s32[]{:T(128)}) while((s32[]{:T(128)}, f32[128,128]{1,0:T(8,128)S(1)}, f32[16,4,8192]{2,0,1:T(8,128)S(1)}, s32[16,8192]{1,0:T(8,128)S(1)}, s32[]{:T(128)}, ...), condition=%wide.region_4.5_spmd.clone, body=%wide.region_3.4_spmd.clone.sunk | while | flops 1613422592 | bytes 11501655 | solution.py:99
  434.3 5.0 fusion.118
  442.1 5.0 fusion.118
  449.9 5.0 fusion.118
  457.7 5.0 fusion.118
  465.5 5.0 fusion.118
  473.3 5.0 fusion.118
  481.1 5.0 fusion.118
  488.9 5.0 fusion.118
  496.7 5.0 fusion.118
  504.5 5.0 fusion.118
  512.3 5.0 fusion.118
  520.1 5.0 fusion.118
  528.0 5.0 fusion.118
  535.8 5.0 fusion.118
  543.6 5.0 fusion.118
  551.4 5.0 fusion.118
  (326 shorter events, 103.3 us)
Async XLA Ops:
  0.6 77.3 %copy-start.10 = (f32[32,128]{1,0:T(8,128)S(1)}, f32[32,128]{1,0:T(8,128)}, u32[]{:S(2)}) copy-start(f32[32,128]{1,0:T(8,128)} %param.18) | copy-start | bytes 49156
  0.6 77.3 %copy-start = (s32[32,128]{1,0:T(8,128)S(1)}, s32[32,128]{1,0:T(8,128)}, u32[]{:S(2)}) copy-start(s32[32,128]{1,0:T(8,128)} %param.20) | copy-start | bytes 49156
  0.7 77.3 %copy-start.11 = (f32[32,128]{1,0:T(8,128)S(1)}, f32[32,128]{1,0:T(8,128)}, u32[]{:S(2)}) copy-start(f32[32,128]{1,0:T(8,128)} %param.19) | copy-start | bytes 49156
  0.7 43.6 %copy-start.14 = (f32[32,128]{1,0:T(8,128)S(1)}, f32[32,128]{1,0:T(8,128)}, u32[]{:S(2)}) copy-start(f32[32,128]{1,0:T(8,128)} %param.17) | copy-start | bytes 49156
  1.4 269.2 %copy-start.5 = (pred[32,128]{1,0:T(8,128)(4,1)}, pred[32,128]{1,0:T(8,128)(4,1)S(1)}, u32[]{:S(2)}) copy-start(pred[32,128]{1,0:T(8,128)(4,1)S(1)} %get-tuple-element.253) | copy-start | bytes 12292
  2.9 11.3 %collective-permute-start = (f32[2,32,1]{2,1,0:T(8,128)}, f32[2,32,1]{2,1,0:T(8,128)S(1)}, u32[]{:S(2)}, u32[]{:S(2)}) collective-permute-start(f32[2,32,1]{2,1,0:T(8,128)} %get-tuple-element.285), channel_id=1, source_target_pairs={{1,0},{2,1},{3,2},{4,3},{5,4},{6,5},{7,6},{8,7},{9,8},{10,9},{11,1... | collective-permute-start | bytes 776 | tf_op jit(solution)/shard_map/ppermute | solution.py:29
  4.2 9.9 %collective-permute-start.1 = (f32[2,32,1]{2,1,0:T(8,128)}, f32[2,32,1]{2,1,0:T(8,128)S(1)}, u32[]{:S(2)}, u32[]{:S(2)}) collective-permute-start(f32[2,32,1]{2,1,0:T(8,128)} %get-tuple-element.284), channel_id=1, source_target_pairs={{0,1},{1,2},{2,3},{3,4},{4,5},{5,6},{6,7},{7,8},{8,9},{9,10},{10,1... | collective-permute-start | bytes 776 | tf_op jit(solution)/shard_map/ppermute | solution.py:26
  7.9 229.0 %copy-start.2 = (f32[1,32,128]{2,1,0:T(8,128)}, f32[1,32,128]{2,1,0:T(8,128)S(1)}, u32[]{:S(2)}) copy-start(f32[1,32,128]{2,1,0:T(8,128)S(1)} %convert_bitcast_fusion) | copy-start | bytes 49156
  9.6 37.8 %collective-permute-start.32 = (f32[9,32,1]{2,1,0:T(8,128)}, f32[9,32,1]{2,1,0:T(8,128)S(1)}, u32[]{:S(2)}, u32[]{:S(2)}) collective-permute-start(f32[9,32,1]{2,1,0:T(8,128)} %get-tuple-element.260), channel_id=1, source_target_pairs={{0,1},{1,2},{2,3},{3,4},{4,5},{5,6},{6,7},{7,8},{8,9},{9,10},{10,1... | collective-permute-start | bytes 3464 | tf_op jit(solution)/shard_map/ppermute | solution.py:26
  10.1 37.3 %collective-permute-start.33 = (f32[9,32,1]{2,1,0:T(8,128)S(1)}, f32[9,32,1]{2,1,0:T(8,128)S(1)}, u32[]{:S(2)}, u32[]{:S(2)}) collective-permute-start(f32[9,32,1]{2,1,0:T(8,128)S(1)} %get-tuple-element.261), channel_id=1, source_target_pairs={{1,0},{2,1},{3,2},{4,3},{5,4},{6,5},{7,6},{8,7},{9,8},{10,9},{11,1... | collective-permute-start | bytes 3464 | tf_op jit(solution)/shard_map/ppermute | solution.py:29
  12.2 187.0 %copy-start.15 = (f32[32]{0:T(128)}, f32[32]{0:T(128)S(1)}, u32[]{:S(2)}) copy-start(f32[32]{0:T(128)S(1)} %cosine_multiply_fusion) | copy-start | bytes 388
  14.3 30.0 %collective-permute-start.3 = (f32[2,1,130]{2,1,0:T(1,128)S(1)}, f32[2,1,130]{2,1,0:T(1,128)S(1)}, u32[]{:S(2)}, u32[]{:S(2)}) collective-permute-start(f32[2,1,130]{2,1,0:T(1,128)S(1)} %get-tuple-element.269), channel_id=1, source_target_pairs={{0,16},{16,32},{32,48},{48,64},{64,80},{80,96},{96,112},{1,17},{17... | collective-permute-start | bytes 3128 | tf_op jit(solution)/shard_map/ppermute | solution.py:26
  18.1 26.2 %collective-permute-start.2 = (f32[2,1,130]{2,1,0:T(1,128)S(1)}, f32[2,1,130]{2,1,0:T(1,128)S(1)}, u32[]{:S(2)}, u32[]{:S(2)}) collective-permute-start(f32[2,1,130]{2,1,0:T(1,128)S(1)} %get-tuple-element.268), channel_id=1, source_target_pairs={{16,0},{32,16},{48,32},{64,48},{80,64},{96,80},{112,96},{17,1},{33... | collective-permute-start | bytes 3128 | tf_op jit(solution)/shard_map/ppermute | solution.py:29
  44.5 3.8 collective-permute-start.4
  47.4 4.7 collective-permute-start.5
  52.1 25.7 %collective-permute-start.6 = (f32[1,1,130]{2,1,0:T(1,128)S(1)}, f32[1,1,130]{2,1,0:T(1,128)S(1)}, u32[]{:S(2)}, u32[]{:S(2)}) collective-permute-start(f32[1,1,130]{2,1,0:T(1,128)S(1)} %get-tuple-element.276), channel_id=1, source_target_pairs={{0,16},{16,32},{32,48},{48,64},{64,80},{80,96},{96,112},{1,17},{17... | collective-permute-start | bytes 1568 | tf_op jit(solution)/shard_map/ppermute | solution.py:26
  56.7 21.1 %collective-permute-start.7 = (f32[1,1,130]{2,1,0:T(1,128)S(1)}, f32[1,1,130]{2,1,0:T(1,128)S(1)}, u32[]{:S(2)}, u32[]{:S(2)}) collective-permute-start(f32[1,1,130]{2,1,0:T(1,128)S(1)} %get-tuple-element.277), channel_id=1, source_target_pairs={{16,0},{32,16},{48,32},{64,48},{80,64},{96,80},{112,96},{17,1},{33... | collective-permute-start | bytes 1568 | tf_op jit(solution)/shard_map/ppermute | solution.py:29
  78.1 8.4 %collective-permute-start.8 = (f32[2,32,1]{2,1,0:T(8,128)S(1)}, f32[2,32,1]{2,1,0:T(8,128)S(1)}, u32[]{:S(2)}, u32[]{:S(2)}) collective-permute-start(f32[2,32,1]{2,1,0:T(8,128)S(1)} %get-tuple-element.283), channel_id=1, source_target_pairs={{1,0},{2,1},{3,2},{4,3},{5,4},{6,5},{7,6},{8,7},{9,8},{10,9},{11,1... | collective-permute-start | bytes 776 | tf_op jit(solution)/shard_map/ppermute | solution.py:29
  78.5 8.0 %collective-permute-start.9 = (f32[2,32,1]{2,1,0:T(8,128)S(1)}, f32[2,32,1]{2,1,0:T(8,128)S(1)}, u32[]{:S(2)}, u32[]{:S(2)}) collective-permute-start(f32[2,32,1]{2,1,0:T(8,128)S(1)} %get-tuple-element.282), channel_id=1, source_target_pairs={{0,1},{1,2},{2,3},{3,4},{4,5},{5,6},{6,7},{7,8},{8,9},{9,10},{10,1... | collective-permute-start | bytes 776 | tf_op jit(solution)/shard_map/ppermute | solution.py:26
  81.4 155.5 %collective-permute-start.34 = (f32[9,1,130]{2,1,0:T(1,128)}, f32[9,1,130]{2,1,0:T(1,128)S(1)}, u32[]{:S(2)}, u32[]{:S(2)}) collective-permute-start(f32[9,1,130]{2,1,0:T(1,128)} %get-tuple-element.258), channel_id=1, source_target_pairs={{0,16},{16,32},{32,48},{48,64},{64,80},{80,96},{96,112},{1,17},{17... | collective-permute-start | bytes 14048 | tf_op jit(solution)/shard_map/ppermute | solution.py:26
  86.6 25.9 %collective-permute-start.11 = (f32[2,1,130]{2,1,0:T(1,128)S(1)}, f32[2,1,130]{2,1,0:T(1,128)S(1)}, u32[]{:S(2)}, u32[]{:S(2)}) collective-permute-start(f32[2,1,130]{2,1,0:T(1,128)S(1)} %get-tuple-element.267), channel_id=1, source_target_pairs={{0,16},{16,32},{32,48},{48,64},{64,80},{80,96},{96,112},{1,17},{17... | collective-permute-start | bytes 3128 | tf_op jit(solution)/shard_map/ppermute | solution.py:26
  90.3 22.2 %collective-permute-start.10 = (f32[2,1,130]{2,1,0:T(1,128)S(1)}, f32[2,1,130]{2,1,0:T(1,128)S(1)}, u32[]{:S(2)}, u32[]{:S(2)}) collective-permute-start(f32[2,1,130]{2,1,0:T(1,128)S(1)} %get-tuple-element.266), channel_id=1, source_target_pairs={{16,0},{32,16},{48,32},{64,48},{80,64},{96,80},{112,96},{17,1},{33... | collective-permute-start | bytes 3128 | tf_op jit(solution)/shard_map/ppermute | solution.py:29
  112.7 4.1 collective-permute-start.12
  115.9 4.7 collective-permute-start.13
  120.7 25.3 %collective-permute-start.14 = (f32[1,1,130]{2,1,0:T(1,128)S(1)}, f32[1,1,130]{2,1,0:T(1,128)S(1)}, u32[]{:S(2)}, u32[]{:S(2)}) collective-permute-start(f32[1,1,130]{2,1,0:T(1,128)S(1)} %get-tuple-element.274), channel_id=1, source_target_pairs={{0,16},{16,32},{32,48},{48,64},{64,80},{80,96},{96,112},{1,17},{17... | collective-permute-start | bytes 1568 | tf_op jit(solution)/shard_map/ppermute | solution.py:26
  125.2 20.8 %collective-permute-start.15 = (f32[1,1,130]{2,1,0:T(1,128)S(1)}, f32[1,1,130]{2,1,0:T(1,128)S(1)}, u32[]{:S(2)}, u32[]{:S(2)}) collective-permute-start(f32[1,1,130]{2,1,0:T(1,128)S(1)} %get-tuple-element.275), channel_id=1, source_target_pairs={{16,0},{32,16},{48,32},{64,48},{80,64},{96,80},{112,96},{17,1},{33... | collective-permute-start | bytes 1568 | tf_op jit(solution)/shard_map/ppermute | solution.py:29
  146.3 23.1 %collective-permute-start.16 = (f32[2,32,1]{2,1,0:T(8,128)S(1)}, f32[2,32,1]{2,1,0:T(8,128)S(1)}, u32[]{:S(2)}, u32[]{:S(2)}) collective-permute-start(f32[2,32,1]{2,1,0:T(8,128)S(1)} %get-tuple-element.281), channel_id=1, source_target_pairs={{1,0},{2,1},{3,2},{4,3},{5,4},{6,5},{7,6},{8,7},{9,8},{10,9},{11,1... | collective-permute-start | bytes 776 | tf_op jit(solution)/shard_map/ppermute | solution.py:29
  146.6 22.7 %collective-permute-start.17 = (f32[2,32,1]{2,1,0:T(8,128)S(1)}, f32[2,32,1]{2,1,0:T(8,128)S(1)}, u32[]{:S(2)}, u32[]{:S(2)}) collective-permute-start(f32[2,32,1]{2,1,0:T(8,128)S(1)} %get-tuple-element.280), channel_id=1, source_target_pairs={{0,1},{1,2},{2,3},{3,4},{4,5},{5,6},{6,7},{7,8},{8,9},{9,10},{10,1... | collective-permute-start | bytes 776 | tf_op jit(solution)/shard_map/ppermute | solution.py:26
  169.5 29.0 %collective-permute-start.19 = (f32[2,1,130]{2,1,0:T(1,128)S(1)}, f32[2,1,130]{2,1,0:T(1,128)}, u32[]{:S(2)}, u32[]{:S(2)}) collective-permute-start(f32[2,1,130]{2,1,0:T(1,128)S(1)} %get-tuple-element.265), channel_id=1, source_target_pairs={{0,16},{16,32},{32,48},{48,64},{64,80},{80,96},{96,112},{1,17},{17... | collective-permute-start | bytes 3128 | tf_op jit(solution)/shard_map/ppermute | solution.py:26
  175.8 22.6 %collective-permute-start.18 = (f32[2,1,130]{2,1,0:T(1,128)S(1)}, f32[2,1,130]{2,1,0:T(1,128)S(1)}, u32[]{:S(2)}, u32[]{:S(2)}) collective-permute-start(f32[2,1,130]{2,1,0:T(1,128)S(1)} %get-tuple-element.264), channel_id=1, source_target_pairs={{16,0},{32,16},{48,32},{64,48},{80,64},{96,80},{112,96},{17,1},{33... | collective-permute-start | bytes 3128 | tf_op jit(solution)/shard_map/ppermute | solution.py:29
  199.3 2.8 collective-permute-start.20
  200.8 5.0 collective-permute-start.21
  200.8 31.8 %collective-permute-start.35 = (f32[9,1,130]{2,1,0:T(1,128)}, f32[9,1,130]{2,1,0:T(1,128)S(1)}, u32[]{:S(2)}, u32[]{:S(2)}) collective-permute-start(f32[9,1,130]{2,1,0:T(1,128)} %get-tuple-element.259), channel_id=1, source_target_pairs={{16,0},{32,16},{48,32},{64,48},{80,64},{96,80},{112,96},{17,1},{33... | collective-permute-start | bytes 14048 | tf_op jit(solution)/shard_map/ppermute | solution.py:29
  205.8 26.8 %collective-permute-start.22 = (f32[1,1,130]{2,1,0:T(1,128)S(1)}, f32[1,1,130]{2,1,0:T(1,128)S(1)}, u32[]{:S(2)}, u32[]{:S(2)}) collective-permute-start(f32[1,1,130]{2,1,0:T(1,128)S(1)} %get-tuple-element.272), channel_id=1, source_target_pairs={{0,16},{16,32},{32,48},{48,64},{64,80},{80,96},{96,112},{1,17},{17... | collective-permute-start | bytes 1568 | tf_op jit(solution)/shard_map/ppermute | solution.py:26
  210.4 22.3 %collective-permute-start.23 = (f32[1,1,130]{2,1,0:T(1,128)S(1)}, f32[1,1,130]{2,1,0:T(1,128)S(1)}, u32[]{:S(2)}, u32[]{:S(2)}) collective-permute-start(f32[1,1,130]{2,1,0:T(1,128)S(1)} %get-tuple-element.273), channel_id=1, source_target_pairs={{16,0},{32,16},{48,32},{64,48},{80,64},{96,80},{112,96},{17,1},{33... | collective-permute-start | bytes 1568 | tf_op jit(solution)/shard_map/ppermute | solution.py:29
  232.6 38.0 %copy-start.7 = (f32[9,1,130]{2,1,0:T(1,128)}, f32[9,1,130]{2,1,0:T(1,128)S(1)}, u32[]{:S(2)}) copy-start(f32[9,1,130]{2,1,0:T(1,128)S(1)} %broadcast_select_fusion) | copy-start | bytes 14044
  233.5 40.6 %copy-start.3 = (f32[32,128]{1,0:T(8,128)}, f32[32,128]{1,0:T(8,128)S(1)}, u32[]{:S(2)}) copy-start(f32[32,128]{1,0:T(8,128)S(1)} %get-tuple-element.246) | copy-start | bytes 49156
  233.5 40.6 %copy-start.4 = (f32[32,128]{1,0:T(8,128)}, f32[32,128]{1,0:T(8,128)S(1)}, u32[]{:S(2)}) copy-start(f32[32,128]{1,0:T(8,128)S(1)} %get-tuple-element.247) | copy-start | bytes 49156
  233.6 4.9 collective-permute-start.24
  234.0 4.5 collective-permute-start.25
  236.9 37.2 %copy-start.13 = (f32[9,1,130]{2,1,0:T(1,128)}, f32[9,1,130]{2,1,0:T(1,128)S(1)}, u32[]{:S(2)}) copy-start(f32[9,1,130]{2,1,0:T(1,128)S(1)} %collective-permute-done.34) | copy-start | bytes 14044
  238.6 32.1 %collective-permute-start.27 = (f32[2,1,130]{2,1,0:T(1,128)S(1)}, f32[2,1,130]{2,1,0:T(1,128)S(1)}, u32[]{:S(2)}, u32[]{:S(2)}) collective-permute-start(f32[2,1,130]{2,1,0:T(1,128)S(1)} %get-tuple-element.263), channel_id=1, source_target_pairs={{0,16},{16,32},{32,48},{48,64},{64,80},{80,96},{96,112},{1,17},{17... | collective-permute-start | bytes 3128 | tf_op jit(solution)/shard_map/ppermute | solution.py:26
  245.2 25.4 %collective-permute-start.26 = (f32[2,1,130]{2,1,0:T(1,128)S(1)}, f32[2,1,130]{2,1,0:T(1,128)S(1)}, u32[]{:S(2)}, u32[]{:S(2)}) collective-permute-start(f32[2,1,130]{2,1,0:T(1,128)S(1)} %get-tuple-element.262), channel_id=1, source_target_pairs={{16,0},{32,16},{48,32},{64,48},{80,64},{96,80},{112,96},{17,1},{33... | collective-permute-start | bytes 3128 | tf_op jit(solution)/shard_map/ppermute | solution.py:29
  270.7 43.4 %copy-start.1 = (f32[32,128]{1,0:T(8,128)}, f32[32,128]{1,0:T(8,128)S(1)}, u32[]{:S(2)}) copy-start(f32[32,128]{1,0:T(8,128)S(1)} %fusion.42) | copy-start | bytes 49156
  270.8 4.2 collective-permute-start.28
  274.1 4.7 collective-permute-start.29
  278.8 0.6 copy-start.12
  280.1 30.2 %collective-permute-start.30 = (f32[1,1,130]{2,1,0:T(1,128)}, f32[1,1,130]{2,1,0:T(1,128)}, u32[]{:S(2)}, u32[]{:S(2)}) collective-permute-start(f32[1,1,130]{2,1,0:T(1,128)} %get-tuple-element.270), channel_id=1, source_target_pairs={{0,16},{16,32},{32,48},{48,64},{64,80},{80,96},{96,112},{1,17},{17... | collective-permute-start | bytes 1568 | tf_op jit(solution)/shard_map/ppermute | solution.py:26
  289.4 21.0 %collective-permute-start.31 = (f32[1,1,130]{2,1,0:T(1,128)}, f32[1,1,130]{2,1,0:T(1,128)S(1)}, u32[]{:S(2)}, u32[]{:S(2)}) collective-permute-start(f32[1,1,130]{2,1,0:T(1,128)} %get-tuple-element.271), channel_id=1, source_target_pairs={{16,0},{32,16},{48,32},{64,48},{80,64},{96,80},{112,96},{17,1},{33... | collective-permute-start | bytes 1568 | tf_op jit(solution)/shard_map/ppermute | solution.py:29
  312.0 1.5 copy-start.9
  312.0 2.2 copy-start.8
  313.4 0.7 copy-start.6
  382.2 45.0 %all-to-all-start = ((f32[4,128,1024]{2,0,1:T(4,128)}), f32[4,128,1024]{2,0,1:T(4,128)S(1)}, u32[]{:S(2)}, u32[]{:S(2)}) async-start(f32[4,128,1024]{2,0,1:T(4,128)} %copy.26), calls=%async_computation | async-start | bytes 4194304 | tf_op jit(solution)/shard_map/all_to_all | solution.py:180
where the time goes:
time: 559 us; the launch traced here: 557 us
  blocking collectives  191 us (34%)
  matrix products  139 us (25%)
  starting transfers between devices  97 us (17%)
  other arithmetic  59.9 us (11%)
  waiting for transfers between devices  45.9 us (8%)
  local copies, waits for them, and re-layouts  21.1 us (4%)
    all_gather x9, blocking collectives, widen(): collected = lax.all_gather(upper[None], 'lon', axis=0, tiled=True)  191 us
    dot_general x16, matrix products, add_block(): lax.dot_general(weighted, low_hot, (((0,), (0,)), ((), ())), precision=la...  79.6 us
    ppermute x18, starting transfers between devices, with_halo(): lax.ppermute(lax.slice_in_dim(block, block.shape[dim] - width, None, axis...  66.6 us
    dot_general x16, matrix products, one_block(): jnp.dot(column_hot, table, precision=lax.Precision.HIGHEST, preferred_ele...  59.5 us
    mul x16, other arithmetic, add_block(): jnp.transpose(value_block)[:, :, None] * high_hot[:, None, :]  39.1 us
    all_to_all x1, waiting for transfers between devices, local(): lax.all_to_all(values, ('lat', 'lon'), split_axis=1, concat_axis=1, tiled...  29 us
    ppermute x18, waiting for transfers between devices, with_halo(): lax.ppermute(lax.slice_in_dim(block, 0, width, axis=dim), axis, backward)  15.9 us
    ppermute x18, starting transfers between devices, with_halo(): lax.ppermute(lax.slice_in_dim(block, 0, width, axis=dim), axis, backward)  15.6 us
  transfers between devices with their start and end apart: 37, of which 8 were waited for; matrix products, arithmetic and copies ran while one was open for 3% of the time, Pallas kernels for 0%

commit v1 on v0

--- a/solution.py
+++ b/solution.py
@@ -37,7 +37,9 @@
     both_wide = with_halo(lon_wide, (("lat", 1),), width, False)
     upper = jnp.flip(lon_wide[:, rows - width :, :], axis=(1, 2))
     sectors = lax.axis_size("lon")
-    collected = lax.all_gather(upper[None], "lon", axis=0, tiled=True)
+    collected = jnp.concatenate(
+        lax.all_to_all(jnp.stack([upper[None]] * lax.axis_size("lon")), "lon", 0, 0), axis=0
+    )
     mirrored = lax.dynamic_index_in_dim(
         collected, sectors - 1 - lax.axis_index("lon"), 0, keepdims=False
     )

time: 559 us -> 484 us (0.87)
  blocking collectives: 191 us -> 0 us
  starting transfers between devices: 97 us -> 184 us
  local copies, waits for them, and re-layouts: 21.1 us -> 39.6 us
  waiting for transfers between devices: 45.9 us -> 61.8 us
  other arithmetic: 59.9 us -> 54 us
    all_gather x9 -> x0, blocking collectives: 191 us -> none  [widen(): collected = lax.all_gather(upper[None], 'lon', axis=0, tiled=True)]
    all_to_all x0 -> x9, starting transfers between devices: none -> 70 us  [widen(): lax.all_to_all(jnp.stack([upper[None]] * lax.axis_size('lon')), 'lon', 0, 0)]
    dynamic_slice x32, local copies, waits for them, and re-layouts: 0.98 us -> 16.2 us  [pick_cells(): picked = lax.map(one_block, blocks).reshape(total, fields_count)]
    ppermute x18, starting transfers between devices: 66.6 us -> 80.5 us  [with_halo(): lax.ppermute(lax.slice_in_dim(block, block.shape[dim] - width, None, axis...]
    all_to_all x0 -> x9, waiting for transfers between devices: none -> 9.73 us  [widen(): lax.all_to_all(jnp.stack([upper[None]] * lax.axis_size('lon')), 'lon', 0, 0)]
    another operation x0 -> x9, local copies, waits for them, and re-layouts: none -> 5.78 us  [widen(): jnp.stack([upper[None]] * lax.axis_size('lon'))]
    ppermute x18, waiting for transfers between devices: 0.96 us -> 6.66 us  [with_halo(): lax.ppermute(lax.slice_in_dim(block, block.shape[dim] - width, None, axis...]
  transfers between devices with their start and end apart: 37 -> 46, of which waited for: 8 -> 21; matrix products, arithmetic and copies ran while one was open for 3% -> 3% of each run, Pallas kernels for 0% -> 0%
where the time goes in v1:
time: 484 us; the launch traced here: 482 us
  starting transfers between devices  184 us (38%)
  matrix products  139 us (29%)
  waiting for transfers between devices  61.8 us (13%)
  other arithmetic  54 us (11%)
  local copies, waits for them, and re-layouts  39.6 us (8%)
    ppermute x18, starting transfers between devices, with_halo(): lax.ppermute(lax.slice_in_dim(block, block.shape[dim] - width, None, axis...  80.5 us
    dot_general x16, matrix products, add_block(): lax.dot_general(weighted, low_hot, (((0,), (0,)), ((), ())), precision=la...  79.6 us
    all_to_all x9, starting transfers between devices, widen(): lax.all_to_all(jnp.stack([upper[None]] * lax.axis_size('lon')), 'lon', 0, 0)  70 us
    dot_general x16, matrix products, one_block(): jnp.dot(column_hot, table, precision=lax.Precision.HIGHEST, preferred_ele...  59.5 us
    mul x16, other arithmetic, add_block(): jnp.transpose(value_block)[:, :, None] * high_hot[:, None, :]  39.8 us
    all_to_all x1, waiting for transfers between devices, local(): lax.all_to_all(values, ('lat', 'lon'), split_axis=1, concat_axis=1, tiled...  28.4 us
    all_to_all x1, starting transfers between devices, local(): lax.all_to_all(values, ('lat', 'lon'), split_axis=1, concat_axis=1, tiled...  19 us
    ppermute x18, waiting for transfers between devices, with_halo(): lax.ppermute(lax.slice_in_dim(block, 0, width, axis=dim), axis, backward)  17 us
  transfers between devices with their start and end apart: 46, of which 21 were waited for; matrix products, arithmetic and copies ran while one was open for 3% of the time, Pallas kernels for 0%

profile of v1, /device:TPU:1, one launch (start us, length us, event | category | flops | bytes accessed | tf_op | source)
XLA Modules:
  0.0 481.6 jit_solution(2303744628994002233)
XLA Ops:
  10.3 9.5 %all-to-all-start = ((f32[16,1,2,1,130]{4,3,2,1,0:T(1,128)}), f32[16,1,2,1,130]{4,3,2,1,0:T(1,128)S(1)}, u32[]{:S(2)}, u32[]{:S(2)}) async-start(f32[16,1,2,1,130]{4,3,2,1,0:T(1,128)} %stack.70), calls=%async_computation | async-start | bytes 65536 | tf_op jit(solution)/shard_map/all_to_all | solution.py:41
  21.1 4.2 collective-permute-start.3
  31.9 3.8 collective-permute-done.5
  36.6 6.3 %all-to-all-start.1 = ((f32[16,1,1,1,130]{4,3,2,1,0:T(1,128)}), f32[16,1,1,1,130]{4,3,2,1,0:T(1,128)S(1)}, u32[]{:S(2)}, u32[]{:S(2)}) async-start(f32[16,1,1,1,130]{4,3,2,1,0:T(1,128)} %stack.71), calls=%async_computation.1 | async-start | bytes 32768 | tf_op jit(solution)/shard_map/all_to_all | solution.py:41
  44.2 4.2 collective-permute-start.6
  57.3 9.5 %all-to-all-start.2 = ((f32[16,1,2,1,130]{4,3,2,1,0:T(1,128)}), f32[16,1,2,1,130]{4,3,2,1,0:T(1,128)S(1)}, u32[]{:S(2)}, u32[]{:S(2)}) async-start(f32[16,1,2,1,130]{4,3,2,1,0:T(1,128)} %stack.75), calls=%async_computation.2 | async-start | bytes 65536 | tf_op jit(solution)/shard_map/all_to_all | solution.py:41
  69.0 3.1 collective-permute-start.32
  72.1 4.3 collective-permute-start.11
  77.2 4.1 collective-permute-start.12
  82.2 4.1 collective-permute-done.13
  87.3 7.7 %all-to-all-start.3 = ((f32[16,1,1,1,130]{4,3,2,1,0:T(1,128)}), f32[16,1,1,1,130]{4,3,2,1,0:T(1,128)S(1)}, u32[]{:S(2)}, u32[]{:S(2)}) async-start(f32[16,1,1,1,130]{4,3,2,1,0:T(1,128)} %stack.76), calls=%async_computation.3 | async-start | bytes 32768 | tf_op jit(solution)/shard_map/all_to_all | solution.py:41
  96.2 5.5 %collective-permute-start.14 = (f32[1,1,130]{2,1,0:T(1,128)S(1)}, f32[1,1,130]{2,1,0:T(1,128)S(1)}, u32[]{:S(2)}, u32[]{:S(2)}) collective-permute-start(f32[1,1,130]{2,1,0:T(1,128)S(1)} %get-tuple-element.298), channel_id=1, source_target_pairs={{0,16},{16,32},{32,48},{48,64},{64,80},{80,96},{96,112},{1,17},{17... | collective-permute-start | bytes 1568 | tf_op jit(solution)/shard_map/ppermute | solution.py:26
  109.9 9.5 %all-to-all-start.4 = ((f32[16,1,2,1,130]{4,3,2,1,0:T(1,128)}), f32[16,1,2,1,130]{4,3,2,1,0:T(1,128)S(1)}, u32[]{:S(2)}, u32[]{:S(2)}) async-start(f32[16,1,2,1,130]{4,3,2,1,0:T(1,128)} %stack.80), calls=%async_computation.4 | async-start | bytes 65536 | tf_op jit(solution)/shard_map/all_to_all | solution.py:41
  120.8 7.2 %collective-permute-start.34 = (f32[9,1,130]{2,0,1:T(8,128)S(1)}, f32[9,1,130]{2,0,1:T(8,128)S(1)}, u32[]{:S(2)}, u32[]{:S(2)}) collective-permute-start(f32[9,1,130]{2,0,1:T(8,128)S(1)} %get-tuple-element.282), channel_id=1, source_target_pairs={{0,16},{16,32},{32,48},{48,64},{64,80},{80,96},{96,112},{1,17},{17... | collective-permute-start | bytes 14048 | tf_op jit(solution)/shard_map/ppermute | solution.py:26
  128.0 5.8 %collective-permute-start.19 = (f32[2,1,130]{2,1,0:T(1,128)S(1)}, f32[2,1,130]{2,1,0:T(1,128)S(1)}, u32[]{:S(2)}, u32[]{:S(2)}) collective-permute-start(f32[2,1,130]{2,1,0:T(1,128)S(1)} %get-tuple-element.289), channel_id=1, source_target_pairs={{0,16},{16,32},{32,48},{48,64},{64,80},{80,96},{96,112},{1,17},{17... | collective-permute-start | bytes 3128 | tf_op jit(solution)/shard_map/ppermute | solution.py:26
  134.7 4.3 collective-permute-start.20
  139.9 3.8 collective-permute-done.21
  144.6 5.9 %all-to-all-start.5 = ((f32[16,1,1,1,130]{4,3,2,1,0:T(1,128)}), f32[16,1,1,1,130]{4,3,2,1,0:T(1,128)S(1)}, u32[]{:S(2)}, u32[]{:S(2)}) async-start(f32[16,1,1,1,130]{4,3,2,1,0:T(1,128)} %stack.81), calls=%async_computation.5 | async-start | bytes 32768 | tf_op jit(solution)/shard_map/all_to_all | solution.py:41
  153.2 7.9 %collective-permute-start.22 = (f32[1,1,130]{2,1,0:T(1,128)S(1)}, f32[1,1,130]{2,1,0:T(1,128)S(1)}, u32[]{:S(2)}, u32[]{:S(2)}) collective-permute-start(f32[1,1,130]{2,1,0:T(1,128)S(1)} %get-tuple-element.296), channel_id=1, source_target_pairs={{0,16},{16,32},{32,48},{48,64},{64,80},{80,96},{96,112},{1,17},{17... | collective-permute-start | bytes 1568 | tf_op jit(solution)/shard_map/ppermute | solution.py:26
  161.8 7.5 %all-to-all-start.8 = ((f32[16,1,9,1,130]{4,3,2,1,0:T(1,128)}), f32[16,1,9,1,130]{4,3,2,1,0:T(1,128)S(1)}, u32[]{:S(2)}, u32[]{:S(2)}) async-start(f32[16,1,9,1,130]{4,3,2,1,0:T(1,128)} %stack.87), calls=%async_computation.8 | async-start | bytes 294912 | tf_op jit(solution)/shard_map/all_to_all | solution.py:41
  169.8 3.1 collective-permute-start.25
  172.9 4.2 all-to-all-done.8
  178.2 8.1 %all-to-all-start.6 = ((f32[16,1,2,1,130]{4,3,2,1,0:T(1,128)}), f32[16,1,2,1,130]{4,3,2,1,0:T(1,128)S(1)}, u32[]{:S(2)}, u32[]{:S(2)}) async-start(f32[16,1,2,1,130]{4,3,2,1,0:T(1,128)} %stack.85), calls=%async_computation.6 | async-start | bytes 65536 | tf_op jit(solution)/shard_map/all_to_all | solution.py:41
  187.7 6.4 %collective-permute-start.27 = (f32[2,1,130]{2,1,0:T(1,128)S(1)}, f32[2,1,130]{2,1,0:T(1,128)S(1)}, u32[]{:S(2)}, u32[]{:S(2)}) collective-permute-start(f32[2,1,130]{2,1,0:T(1,128)S(1)} %get-tuple-element.287), channel_id=1, source_target_pairs={{0,16},{16,32},{32,48},{48,64},{64,80},{80,96},{96,112},{1,17},{17... | collective-permute-start | bytes 3128 | tf_op jit(solution)/shard_map/ppermute | solution.py:26
  195.0 4.0 collective-permute-start.28
  199.9 3.8 collective-permute-done.29
  204.7 5.9 %all-to-all-start.7 = ((f32[16,1,1,1,130]{4,3,2,1,0:T(1,128)}), f32[16,1,1,1,130]{4,3,2,1,0:T(1,128)S(1)}, u32[]{:S(2)}, u32[]{:S(2)}) async-start(f32[16,1,1,1,130]{4,3,2,1,0:T(1,128)} %stack.86), calls=%async_computation.7 | async-start | bytes 32768 | tf_op jit(solution)/shard_map/all_to_all | solution.py:41
  212.0 4.5 collective-permute-start.30
  219.7 78.1 %while.26 = (s32[]{:T(128)}, f32[16,8192,4]{1,2,0:T(4,128)S(1)}, s32[16,8192]{1,0:T(8,128)}, f32[128,128]{1,0:T(8,128)S(1)}, s32[]{:T(128)}) while((s32[]{:T(128)}, f32[16,8192,4]{1,2,0:T(4,128)S(1)}, s32[16,8192]{1,0:T(8,128)}, f32[128,128]{1,0:T(8,128)S(1)}, s32[]{:T(128)}) %tuple.101), condition=%wide.region_2.3_spmd.clone, body=%wide.region_0.2_spmd.clone.sunk | while | flops 1614405632 | bytes 2785349 | solution.py:70
  220.9 3.7 multiply_reduce_fusion.2
  225.7 3.7 multiply_reduce_fusion.2
  230.6 3.7 multiply_reduce_fusion.2
  235.5 3.7 multiply_reduce_fusion.2
  240.4 3.7 multiply_reduce_fusion.2
  245.2 3.7 multiply_reduce_fusion.2
  250.1 3.7 multiply_reduce_fusion.2
  255.0 3.7 multiply_reduce_fusion.2
  259.9 3.7 multiply_reduce_fusion.2
  264.8 3.7 multiply_reduce_fusion.2
  269.6 3.7 multiply_reduce_fusion.2
  274.5 3.7 multiply_reduce_fusion.2
  279.4 3.7 multiply_reduce_fusion.2
  284.3 3.7 multiply_reduce_fusion.2
  289.1 3.7 multiply_reduce_fusion.2
  294.0 3.7 multiply_reduce_fusion.2
  301.8 19.0 %all-to-all-start.9 = ((f32[4,128,1024]{2,0,1:T(4,128)}), f32[4,128,1024]{2,0,1:T(4,128)S(1)}, u32[]{:S(2)}, u32[]{:S(2)}) async-start(f32[4,128,1024]{2,0,1:T(4,128)} %copy.50), calls=%async_computation.9 | async-start | bytes 4194304 | tf_op jit(solution)/shard_map/all_to_all | solution.py:182
  322.7 28.4 %all-to-all-done.9 = f32[4,128,1024]{2,0,1:T(4,128)S(1)} async-done(((f32[4,128,1024]{2,0,1:T(4,128)}), f32[4,128,1024]{2,0,1:T(4,128)S(1)}, u32[]{:S(2)}, u32[]{:S(2)}) %all-to-all-start.9) | async-done | bytes 2097184 | tf_op jit(solution)/shard_map/all_to_all | solution.py:182
  355.3 125.6 %while.27 = (s32[]{:T(128)}, f32[128,128]{1,0:T(8,128)S(1)}, f32[16,4,8192]{2,0,1:T(8,128)S(1)}, s32[16,8192]{1,0:T(8,128)S(1)}, s32[]{:T(128)}, /*index=5*/s32[]{:T(128)}) while((s32[]{:T(128)}, f32[128,128]{1,0:T(8,128)S(1)}, f32[16,4,8192]{2,0,1:T(8,128)S(1)}, s32[16,8192]{1,0:T(8,128)S(1)}, s32[]{:T(128)}, ...), condition=%wide.region_4.5_spmd.clone, body=%wide.region_3.4_spmd.clone.sunk | while | flops 1613422592 | bytes 11501655 | solution.py:101
  358.2 5.0 %fusion.120 = f32[128,128]{1,0:T(8,128)S(1)} fusion(f32[8192,128]{0,1:T(8,128)} %bitcast.157, s32[8192]{0:T(1024)S(1)} %get-tuple-element.375, f32[128,128]{1,0:T(8,128)S(1)} %get-tuple-element.398, pred[]{:T(512)S(6)} %compare.31), kind=kOutput, calls=%fused_computation.24.clone.1 | convolution fusion | flops 1611694080 | bytes 4358145 | tf_op jit(solution)/shard_map/while/body/eval_jaxpr/dot_general | solution.py:91
  366.0 5.0 %fusion.120 = f32[128,128]{1,0:T(8,128)S(1)} fusion(f32[8192,128]{0,1:T(8,128)} %bitcast.157, s32[8192]{0:T(1024)S(1)} %get-tuple-element.375, f32[128,128]{1,0:T(8,128)S(1)} %get-tuple-element.398, pred[]{:T(512)S(6)} %compare.31), kind=kOutput, calls=%fused_computation.24.clone.1 | convolution fusion | flops 1611694080 | bytes 4358145 | tf_op jit(solution)/shard_map/while/body/eval_jaxpr/dot_general | solution.py:91
  373.9 5.0 %fusion.120 = f32[128,128]{1,0:T(8,128)S(1)} fusion(f32[8192,128]{0,1:T(8,128)} %bitcast.157, s32[8192]{0:T(1024)S(1)} %get-tuple-element.375, f32[128,128]{1,0:T(8,128)S(1)} %get-tuple-element.398, pred[]{:T(512)S(6)} %compare.31), kind=kOutput, calls=%fused_computation.24.clone.1 | convolution fusion | flops 1611694080 | bytes 4358145 | tf_op jit(solution)/shard_map/while/body/eval_jaxpr/dot_general | solution.py:91
  381.7 5.0 %fusion.120 = f32[128,128]{1,0:T(8,128)S(1)} fusion(f32[8192,128]{0,1:T(8,128)} %bitcast.157, s32[8192]{0:T(1024)S(1)} %get-tuple-element.375, f32[128,128]{1,0:T(8,128)S(1)} %get-tuple-element.398, pred[]{:T(512)S(6)} %compare.31), kind=kOutput, calls=%fused_computation.24.clone.1 | convolution fusion | flops 1611694080 | bytes 4358145 | tf_op jit(solution)/shard_map/while/body/eval_jaxpr/dot_general | solution.py:91
  389.6 5.0 %fusion.120 = f32[128,128]{1,0:T(8,128)S(1)} fusion(f32[8192,128]{0,1:T(8,128)} %bitcast.157, s32[8192]{0:T(1024)S(1)} %get-tuple-element.375, f32[128,128]{1,0:T(8,128)S(1)} %get-tuple-element.398, pred[]{:T(512)S(6)} %compare.31), kind=kOutput, calls=%fused_computation.24.clone.1 | convolution fusion | flops 1611694080 | bytes 4358145 | tf_op jit(solution)/shard_map/while/body/eval_jaxpr/dot_general | solution.py:91
  397.4 5.0 %fusion.120 = f32[128,128]{1,0:T(8,128)S(1)} fusion(f32[8192,128]{0,1:T(8,128)} %bitcast.157, s32[8192]{0:T(1024)S(1)} %get-tuple-element.375, f32[128,128]{1,0:T(8,128)S(1)} %get-tuple-element.398, pred[]{:T(512)S(6)} %compare.31), kind=kOutput, calls=%fused_computation.24.clone.1 | convolution fusion | flops 1611694080 | bytes 4358145 | tf_op jit(solution)/shard_map/while/body/eval_jaxpr/dot_general | solution.py:91
  405.3 5.0 %fusion.120 = f32[128,128]{1,0:T(8,128)S(1)} fusion(f32[8192,128]{0,1:T(8,128)} %bitcast.157, s32[8192]{0:T(1024)S(1)} %get-tuple-element.375, f32[128,128]{1,0:T(8,128)S(1)} %get-tuple-element.398, pred[]{:T(512)S(6)} %compare.31), kind=kOutput, calls=%fused_computation.24.clone.1 | convolution fusion | flops 1611694080 | bytes 4358145 | tf_op jit(solution)/shard_map/while/body/eval_jaxpr/dot_general | solution.py:91
  413.1 5.0 %fusion.120 = f32[128,128]{1,0:T(8,128)S(1)} fusion(f32[8192,128]{0,1:T(8,128)} %bitcast.157, s32[8192]{0:T(1024)S(1)} %get-tuple-element.375, f32[128,128]{1,0:T(8,128)S(1)} %get-tuple-element.398, pred[]{:T(512)S(6)} %compare.31), kind=kOutput, calls=%fused_computation.24.clone.1 | convolution fusion | flops 1611694080 | bytes 4358145 | tf_op jit(solution)/shard_map/while/body/eval_jaxpr/dot_general | solution.py:91
  421.0 5.0 %fusion.120 = f32[128,128]{1,0:T(8,128)S(1)} fusion(f32[8192,128]{0,1:T(8,128)} %bitcast.157, s32[8192]{0:T(1024)S(1)} %get-tuple-element.375, f32[128,128]{1,0:T(8,128)S(1)} %get-tuple-element.398, pred[]{:T(512)S(6)} %compare.31), kind=kOutput, calls=%fused_computation.24.clone.1 | convolution fusion | flops 1611694080 | bytes 4358145 | tf_op jit(solution)/shard_map/while/body/eval_jaxpr/dot_general | solution.py:91
  428.8 5.0 %fusion.120 = f32[128,128]{1,0:T(8,128)S(1)} fusion(f32[8192,128]{0,1:T(8,128)} %bitcast.157, s32[8192]{0:T(1024)S(1)} %get-tuple-element.375, f32[128,128]{1,0:T(8,128)S(1)} %get-tuple-element.398, pred[]{:T(512)S(6)} %compare.31), kind=kOutput, calls=%fused_computation.24.clone.1 | convolution fusion | flops 1611694080 | bytes 4358145 | tf_op jit(solution)/shard_map/while/body/eval_jaxpr/dot_general | solution.py:91
  436.7 5.0 %fusion.120 = f32[128,128]{1,0:T(8,128)S(1)} fusion(f32[8192,128]{0,1:T(8,128)} %bitcast.157, s32[8192]{0:T(1024)S(1)} %get-tuple-element.375, f32[128,128]{1,0:T(8,128)S(1)} %get-tuple-element.398, pred[]{:T(512)S(6)} %compare.31), kind=kOutput, calls=%fused_computation.24.clone.1 | convolution fusion | flops 1611694080 | bytes 4358145 | tf_op jit(solution)/shard_map/while/body/eval_jaxpr/dot_general | solution.py:91
  444.5 5.0 %fusion.120 = f32[128,128]{1,0:T(8,128)S(1)} fusion(f32[8192,128]{0,1:T(8,128)} %bitcast.157, s32[8192]{0:T(1024)S(1)} %get-tuple-element.375, f32[128,128]{1,0:T(8,128)S(1)} %get-tuple-element.398, pred[]{:T(512)S(6)} %compare.31), kind=kOutput, calls=%fused_computation.24.clone.1 | convolution fusion | flops 1611694080 | bytes 4358145 | tf_op jit(solution)/shard_map/while/body/eval_jaxpr/dot_general | solution.py:91
  452.4 5.0 %fusion.120 = f32[128,128]{1,0:T(8,128)S(1)} fusion(f32[8192,128]{0,1:T(8,128)} %bitcast.157, s32[8192]{0:T(1024)S(1)} %get-tuple-element.375, f32[128,128]{1,0:T(8,128)S(1)} %get-tuple-element.398, pred[]{:T(512)S(6)} %compare.31), kind=kOutput, calls=%fused_computation.24.clone.1 | convolution fusion | flops 1611694080 | bytes 4358145 | tf_op jit(solution)/shard_map/while/body/eval_jaxpr/dot_general | solution.py:91
  460.2 5.0 %fusion.120 = f32[128,128]{1,0:T(8,128)S(1)} fusion(f32[8192,128]{0,1:T(8,128)} %bitcast.157, s32[8192]{0:T(1024)S(1)} %get-tuple-element.375, f32[128,128]{1,0:T(8,128)S(1)} %get-tuple-element.398, pred[]{:T(512)S(6)} %compare.31), kind=kOutput, calls=%fused_computation.24.clone.1 | convolution fusion | flops 1611694080 | bytes 4358145 | tf_op jit(solution)/shard_map/while/body/eval_jaxpr/dot_general | solution.py:91
  468.1 5.0 %fusion.120 = f32[128,128]{1,0:T(8,128)S(1)} fusion(f32[8192,128]{0,1:T(8,128)} %bitcast.157, s32[8192]{0:T(1024)S(1)} %get-tuple-element.375, f32[128,128]{1,0:T(8,128)S(1)} %get-tuple-element.398, pred[]{:T(512)S(6)} %compare.31), kind=kOutput, calls=%fused_computation.24.clone.1 | convolution fusion | flops 1611694080 | bytes 4358145 | tf_op jit(solution)/shard_map/while/body/eval_jaxpr/dot_general | solution.py:91
  475.9 5.0 %fusion.120 = f32[128,128]{1,0:T(8,128)S(1)} fusion(f32[8192,128]{0,1:T(8,128)} %bitcast.157, s32[8192]{0:T(1024)S(1)} %get-tuple-element.375, f32[128,128]{1,0:T(8,128)S(1)} %get-tuple-element.398, pred[]{:T(512)S(6)} %compare.31), kind=kOutput, calls=%fused_computation.24.clone.1 | convolution fusion | flops 1611694080 | bytes 4358145 | tf_op jit(solution)/shard_map/while/body/eval_jaxpr/dot_general | solution.py:91
  (334 shorter events, 133.6 us)
Async XLA Ops:
  0.6 102.0 %copy-start = (s32[32,128]{1,0:T(8,128)S(1)}, s32[32,128]{1,0:T(8,128)}, u32[]{:S(2)}) copy-start(s32[32,128]{1,0:T(8,128)} %param.20) | copy-start | bytes 49156
  0.6 80.7 %copy-start.6 = (s32[1,128]{1,0:T(1,128)S(1)}, s32[1,128]{1,0:T(1,128)}, u32[]{:S(2)}) copy-start(s32[1,128]{1,0:T(1,128)} %param.26) | copy-start | bytes 1540
  2.2 5.9 %collective-permute-start = (f32[2,32,1]{2,1,0:T(8,128)S(1)}, f32[2,32,1]{2,1,0:T(8,128)S(1)}, u32[]{:S(2)}, u32[]{:S(2)}) collective-permute-start(f32[2,32,1]{2,1,0:T(8,128)S(1)} %get-tuple-element.309), channel_id=1, source_target_pairs={{1,0},{2,1},{3,2},{4,3},{5,4},{6,5},{7,6},{8,7},{9,8},{10,9},{11,1... | collective-permute-start | bytes 776 | tf_op jit(solution)/shard_map/ppermute | solution.py:29
  3.6 5.6 %collective-permute-start.1 = (f32[2,32,1]{2,1,0:T(8,128)S(1)}, f32[2,32,1]{2,1,0:T(8,128)S(1)}, u32[]{:S(2)}, u32[]{:S(2)}) collective-permute-start(f32[2,32,1]{2,1,0:T(8,128)S(1)} %get-tuple-element.308), channel_id=1, source_target_pairs={{0,1},{1,2},{2,3},{3,4},{4,5},{5,6},{6,7},{7,8},{8,9},{9,10},{10,1... | collective-permute-start | bytes 776 | tf_op jit(solution)/shard_map/ppermute | solution.py:26
  10.3 16.9 %all-to-all-start = ((f32[16,1,2,1,130]{4,3,2,1,0:T(1,128)}), f32[16,1,2,1,130]{4,3,2,1,0:T(1,128)S(1)}, u32[]{:S(2)}, u32[]{:S(2)}) async-start(f32[16,1,2,1,130]{4,3,2,1,0:T(1,128)} %stack.70), calls=%async_computation | async-start | bytes 65536 | tf_op jit(solution)/shard_map/all_to_all | solution.py:41
  19.8 5.5 %collective-permute-start.2 = (f32[2,1,130]{2,1,0:T(1,128)S(1)}, f32[2,1,130]{2,1,0:T(1,128)S(1)}, u32[]{:S(2)}, u32[]{:S(2)}) collective-permute-start(f32[2,1,130]{2,1,0:T(1,128)S(1)} %get-tuple-element.292), channel_id=1, source_target_pairs={{16,0},{32,16},{48,32},{64,48},{80,64},{96,80},{112,96},{17,1},{33... | collective-permute-start | bytes 3128 | tf_op jit(solution)/shard_map/ppermute | solution.py:29
  21.1 6.1 %collective-permute-start.3 = (f32[2,1,130]{2,1,0:T(1,128)S(1)}, f32[2,1,130]{2,1,0:T(1,128)S(1)}, u32[]{:S(2)}, u32[]{:S(2)}) collective-permute-start(f32[2,1,130]{2,1,0:T(1,128)S(1)} %get-tuple-element.293), channel_id=1, source_target_pairs={{0,16},{16,32},{32,48},{48,64},{64,80},{80,96},{96,112},{1,17},{17... | collective-permute-start | bytes 3128 | tf_op jit(solution)/shard_map/ppermute | solution.py:26
  28.1 3.8 collective-permute-start.4
  31.0 4.7 collective-permute-start.5
  36.6 13.6 %all-to-all-start.1 = ((f32[16,1,1,1,130]{4,3,2,1,0:T(1,128)}), f32[16,1,1,1,130]{4,3,2,1,0:T(1,128)S(1)}, u32[]{:S(2)}, u32[]{:S(2)}) async-start(f32[16,1,1,1,130]{4,3,2,1,0:T(1,128)} %stack.71), calls=%async_computation.1 | async-start | bytes 32768 | tf_op jit(solution)/shard_map/all_to_all | solution.py:41
  42.9 5.5 %collective-permute-start.7 = (f32[1,1,130]{2,1,0:T(1,128)S(1)}, f32[1,1,130]{2,1,0:T(1,128)S(1)}, u32[]{:S(2)}, u32[]{:S(2)}) collective-permute-start(f32[1,1,130]{2,1,0:T(1,128)S(1)} %get-tuple-element.301), channel_id=1, source_target_pairs={{16,0},{32,16},{48,32},{64,48},{80,64},{96,80},{112,96},{17,1},{33... | collective-permute-start | bytes 1568 | tf_op jit(solution)/shard_map/ppermute | solution.py:29
  44.2 6.0 %collective-permute-start.6 = (f32[1,1,130]{2,1,0:T(1,128)S(1)}, f32[1,1,130]{2,1,0:T(1,128)S(1)}, u32[]{:S(2)}, u32[]{:S(2)}) collective-permute-start(f32[1,1,130]{2,1,0:T(1,128)S(1)} %get-tuple-element.300), channel_id=1, source_target_pairs={{0,16},{16,32},{32,48},{48,64},{64,80},{80,96},{96,112},{1,17},{17... | collective-permute-start | bytes 1568 | tf_op jit(solution)/shard_map/ppermute | solution.py:26
  51.2 5.0 %collective-permute-start.8 = (f32[2,32,1]{2,1,0:T(8,128)S(1)}, f32[2,32,1]{2,1,0:T(8,128)S(1)}, u32[]{:S(2)}, u32[]{:S(2)}) collective-permute-start(f32[2,32,1]{2,1,0:T(8,128)S(1)} %get-tuple-element.307), channel_id=1, source_target_pairs={{1,0},{2,1},{3,2},{4,3},{5,4},{6,5},{7,6},{8,7},{9,8},{10,9},{11,1... | collective-permute-start | bytes 776 | tf_op jit(solution)/shard_map/ppermute | solution.py:29
  51.6 4.6 collective-permute-start.9
  57.3 19.1 %all-to-all-start.2 = ((f32[16,1,2,1,130]{4,3,2,1,0:T(1,128)}), f32[16,1,2,1,130]{4,3,2,1,0:T(1,128)S(1)}, u32[]{:S(2)}, u32[]{:S(2)}) async-start(f32[16,1,2,1,130]{4,3,2,1,0:T(1,128)} %stack.75), calls=%async_computation.2 | async-start | bytes 65536 | tf_op jit(solution)/shard_map/all_to_all | solution.py:41
  66.8 9.6 %collective-permute-start.10 = (f32[2,1,130]{2,1,0:T(1,128)S(1)}, f32[2,1,130]{2,1,0:T(1,128)S(1)}, u32[]{:S(2)}, u32[]{:S(2)}) collective-permute-start(f32[2,1,130]{2,1,0:T(1,128)S(1)} %get-tuple-element.290), channel_id=1, source_target_pairs={{16,0},{32,16},{48,32},{64,48},{80,64},{96,80},{112,96},{17,1},{33... | collective-permute-start | bytes 3128 | tf_op jit(solution)/shard_map/ppermute | solution.py:29
  69.0 51.7 %collective-permute-start.32 = (f32[9,32,1]{2,0,1:T(8,128)}, f32[9,32,1]{2,0,1:T(8,128)S(1)}, u32[]{:S(2)}, u32[]{:S(2)}) collective-permute-start(f32[9,32,1]{2,0,1:T(8,128)} %get-tuple-element.284), channel_id=1, source_target_pairs={{0,1},{1,2},{2,3},{3,4},{4,5},{5,6},{6,7},{7,8},{8,9},{9,10},{10,1... | collective-permute-start | bytes 3464 | tf_op jit(solution)/shard_map/ppermute | solution.py:26
  72.1 48.6 %collective-permute-start.33 = (f32[9,32,1]{2,0,1:T(8,128)}, f32[9,32,1]{2,0,1:T(8,128)S(1)}, u32[]{:S(2)}, u32[]{:S(2)}) collective-permute-start(f32[9,32,1]{2,0,1:T(8,128)} %get-tuple-element.285), channel_id=1, source_target_pairs={{1,0},{2,1},{3,2},{4,3},{5,4},{6,5},{7,6},{8,7},{9,8},{10,9},{11,1... | collective-permute-start | bytes 3464 | tf_op jit(solution)/shard_map/ppermute | solution.py:29
  72.1 5.0 %collective-permute-start.11 = (f32[2,1,130]{2,1,0:T(1,128)S(1)}, f32[2,1,130]{2,1,0:T(1,128)S(1)}, u32[]{:S(2)}, u32[]{:S(2)}) collective-permute-start(f32[2,1,130]{2,1,0:T(1,128)S(1)} %get-tuple-element.291), channel_id=1, source_target_pairs={{0,16},{16,32},{32,48},{48,64},{64,80},{80,96},{96,112},{1,17},{17... | collective-permute-start | bytes 3128 | tf_op jit(solution)/shard_map/ppermute | solution.py:26
  77.2 5.0 %collective-permute-start.12 = (f32[1,32,1]{2,1,0:T(8,128)S(1)}, f32[1,32,1]{2,1,0:T(8,128)S(1)}, u32[]{:S(2)}, u32[]{:S(2)}) collective-permute-start(f32[1,32,1]{2,1,0:T(8,128)S(1)} %get-tuple-element.314), channel_id=1, source_target_pairs={{0,1},{1,2},{2,3},{3,4},{4,5},{5,6},{6,7},{7,8},{8,9},{9,10},{10,1... | collective-permute-start | bytes 392 | tf_op jit(solution)/shard_map/ppermute | solution.py:26
  81.4 5.0 %collective-permute-start.13 = (f32[1,32,1]{2,1,0:T(8,128)S(1)}, f32[1,32,1]{2,1,0:T(8,128)S(1)}, u32[]{:S(2)}, u32[]{:S(2)}) collective-permute-start(f32[1,32,1]{2,1,0:T(8,128)S(1)} %get-tuple-element.315), channel_id=1, source_target_pairs={{1,0},{2,1},{3,2},{4,3},{5,4},{6,5},{7,6},{8,7},{9,8},{10,9},{11,1... | collective-permute-start | bytes 392 | tf_op jit(solution)/shard_map/ppermute | solution.py:29
  87.3 15.0 %all-to-all-start.3 = ((f32[16,1,1,1,130]{4,3,2,1,0:T(1,128)}), f32[16,1,1,1,130]{4,3,2,1,0:T(1,128)S(1)}, u32[]{:S(2)}, u32[]{:S(2)}) async-start(f32[16,1,1,1,130]{4,3,2,1,0:T(1,128)} %stack.76), calls=%async_computation.3 | async-start | bytes 32768 | tf_op jit(solution)/shard_map/all_to_all | solution.py:41
  95.0 6.8 %collective-permute-start.15 = (f32[1,1,130]{2,1,0:T(1,128)S(1)}, f32[1,1,130]{2,1,0:T(1,128)S(1)}, u32[]{:S(2)}, u32[]{:S(2)}) collective-permute-start(f32[1,1,130]{2,1,0:T(1,128)S(1)} %get-tuple-element.299), channel_id=1, source_target_pairs={{16,0},{32,16},{48,32},{64,48},{80,64},{96,80},{112,96},{17,1},{33... | collective-permute-start | bytes 1568 | tf_op jit(solution)/shard_map/ppermute | solution.py:29
  96.2 6.2 %collective-permute-start.14 = (f32[1,1,130]{2,1,0:T(1,128)S(1)}, f32[1,1,130]{2,1,0:T(1,128)S(1)}, u32[]{:S(2)}, u32[]{:S(2)}) collective-permute-start(f32[1,1,130]{2,1,0:T(1,128)S(1)} %get-tuple-element.298), channel_id=1, source_target_pairs={{0,16},{16,32},{32,48},{48,64},{64,80},{80,96},{96,112},{1,17},{17... | collective-permute-start | bytes 1568 | tf_op jit(solution)/shard_map/ppermute | solution.py:26
  102.8 6.0 %collective-permute-start.16 = (f32[2,32,1]{2,1,0:T(8,128)S(1)}, f32[2,32,1]{2,1,0:T(8,128)S(1)}, u32[]{:S(2)}, u32[]{:S(2)}) collective-permute-start(f32[2,32,1]{2,1,0:T(8,128)S(1)} %get-tuple-element.305), channel_id=1, source_target_pairs={{1,0},{2,1},{3,2},{4,3},{5,4},{6,5},{7,6},{8,7},{9,8},{10,9},{11,1... | collective-permute-start | bytes 776 | tf_op jit(solution)/shard_map/ppermute | solution.py:29
  103.7 5.1 %collective-permute-start.17 = (f32[2,32,1]{2,1,0:T(8,128)S(1)}, f32[2,32,1]{2,1,0:T(8,128)S(1)}, u32[]{:S(2)}, u32[]{:S(2)}) collective-permute-start(f32[2,32,1]{2,1,0:T(8,128)S(1)} %get-tuple-element.304), channel_id=1, source_target_pairs={{0,1},{1,2},{2,3},{3,4},{4,5},{5,6},{6,7},{7,8},{8,9},{9,10},{10,1... | collective-permute-start | bytes 776 | tf_op jit(solution)/shard_map/ppermute | solution.py:26
  108.8 109.4 %copy-start.3 = (f32[8,32,128]{2,1,0:T(8,128)S(1)}, f32[8,32,128]{2,1,0:T(8,128)}, u32[]{:S(2)}) copy-start(f32[8,32,128]{2,1,0:T(8,128)} %param.22) | copy-start | bytes 393220
  109.9 24.0 %all-to-all-start.4 = ((f32[16,1,2,1,130]{4,3,2,1,0:T(1,128)}), f32[16,1,2,1,130]{4,3,2,1,0:T(1,128)S(1)}, u32[]{:S(2)}, u32[]{:S(2)}) async-start(f32[16,1,2,1,130]{4,3,2,1,0:T(1,128)} %stack.80), calls=%async_computation.4 | async-start | bytes 65536 | tf_op jit(solution)/shard_map/all_to_all | solution.py:41
  119.4 14.4 %collective-permute-start.18 = (f32[2,1,130]{2,1,0:T(1,128)S(1)}, f32[2,1,130]{2,1,0:T(1,128)S(1)}, u32[]{:S(2)}, u32[]{:S(2)}) collective-permute-start(f32[2,1,130]{2,1,0:T(1,128)S(1)} %get-tuple-element.288), channel_id=1, source_target_pairs={{16,0},{32,16},{48,32},{64,48},{80,64},{96,80},{112,96},{17,1},{33... | collective-permute-start | bytes 3128 | tf_op jit(solution)/shard_map/ppermute | solution.py:29
  120.8 66.8 %collective-permute-start.34 = (f32[9,1,130]{2,0,1:T(8,128)S(1)}, f32[9,1,130]{2,0,1:T(8,128)S(1)}, u32[]{:S(2)}, u32[]{:S(2)}) collective-permute-start(f32[9,1,130]{2,0,1:T(8,128)S(1)} %get-tuple-element.282), channel_id=1, source_target_pairs={{0,16},{16,32},{32,48},{48,64},{64,80},{80,96},{96,112},{1,17},{17... | collective-permute-start | bytes 14048 | tf_op jit(solution)/shard_map/ppermute | solution.py:26
  128.0 6.5 %collective-permute-start.19 = (f32[2,1,130]{2,1,0:T(1,128)S(1)}, f32[2,1,130]{2,1,0:T(1,128)S(1)}, u32[]{:S(2)}, u32[]{:S(2)}) collective-permute-start(f32[2,1,130]{2,1,0:T(1,128)S(1)} %get-tuple-element.289), channel_id=1, source_target_pairs={{0,16},{16,32},{32,48},{48,64},{64,80},{80,96},{96,112},{1,17},{17... | collective-permute-start | bytes 3128 | tf_op jit(solution)/shard_map/ppermute | solution.py:26
  134.7 5.2 %collective-permute-start.20 = (f32[1,32,1]{2,1,0:T(8,128)S(1)}, f32[1,32,1]{2,1,0:T(8,128)S(1)}, u32[]{:S(2)}, u32[]{:S(2)}) collective-permute-start(f32[1,32,1]{2,1,0:T(8,128)S(1)} %get-tuple-element.312), channel_id=1, source_target_pairs={{0,1},{1,2},{2,3},{3,4},{4,5},{5,6},{6,7},{7,8},{8,9},{9,10},{10,1... | collective-permute-start | bytes 392 | tf_op jit(solution)/shard_map/ppermute | solution.py:26
  139.0 4.7 collective-permute-start.21
  144.6 16.5 %all-to-all-start.5 = ((f32[16,1,1,1,130]{4,3,2,1,0:T(1,128)}), f32[16,1,1,1,130]{4,3,2,1,0:T(1,128)S(1)}, u32[]{:S(2)}, u32[]{:S(2)}) async-start(f32[16,1,1,1,130]{4,3,2,1,0:T(1,128)} %stack.81), calls=%async_computation.5 | async-start | bytes 32768 | tf_op jit(solution)/shard_map/all_to_all | solution.py:41
  150.6 18.8 %collective-permute-start.23 = (f32[1,1,130]{2,1,0:T(1,128)S(1)}, f32[1,1,130]{2,1,0:T(1,128)S(1)}, u32[]{:S(2)}, u32[]{:S(2)}) collective-permute-start(f32[1,1,130]{2,1,0:T(1,128)S(1)} %get-tuple-element.297), channel_id=1, source_target_pairs={{16,0},{32,16},{48,32},{64,48},{80,64},{96,80},{112,96},{17,1},{33... | collective-permute-start | bytes 1568 | tf_op jit(solution)/shard_map/ppermute | solution.py:29
  151.9 25.2 %collective-permute-start.35 = (f32[9,1,130]{2,0,1:T(8,128)S(1)}, f32[9,1,130]{2,0,1:T(8,128)S(1)}, u32[]{:S(2)}, u32[]{:S(2)}) collective-permute-start(f32[9,1,130]{2,0,1:T(8,128)S(1)} %get-tuple-element.283), channel_id=1, source_target_pairs={{16,0},{32,16},{48,32},{64,48},{80,64},{96,80},{112,96},{17,1},{33... | collective-permute-start | bytes 14048 | tf_op jit(solution)/shard_map/ppermute | solution.py:29
  153.2 16.2 %collective-permute-start.22 = (f32[1,1,130]{2,1,0:T(1,128)S(1)}, f32[1,1,130]{2,1,0:T(1,128)S(1)}, u32[]{:S(2)}, u32[]{:S(2)}) collective-permute-start(f32[1,1,130]{2,1,0:T(1,128)S(1)} %get-tuple-element.296), channel_id=1, source_target_pairs={{0,16},{16,32},{32,48},{48,64},{64,80},{80,96},{96,112},{1,17},{17... | collective-permute-start | bytes 1568 | tf_op jit(solution)/shard_map/ppermute | solution.py:26
  161.8 15.3 %all-to-all-start.8 = ((f32[16,1,9,1,130]{4,3,2,1,0:T(1,128)}), f32[16,1,9,1,130]{4,3,2,1,0:T(1,128)S(1)}, u32[]{:S(2)}, u32[]{:S(2)}) async-start(f32[16,1,9,1,130]{4,3,2,1,0:T(1,128)} %stack.87), calls=%async_computation.8 | async-start | bytes 294912 | tf_op jit(solution)/shard_map/all_to_all | solution.py:41
  169.6 7.5 %collective-permute-start.24 = (f32[2,32,1]{2,1,0:T(8,128)S(1)}, f32[2,32,1]{2,1,0:T(8,128)S(1)}, u32[]{:S(2)}, u32[]{:S(2)}) collective-permute-start(f32[2,32,1]{2,1,0:T(8,128)S(1)} %get-tuple-element.303), channel_id=1, source_target_pairs={{1,0},{2,1},{3,2},{4,3},{5,4},{6,5},{7,6},{8,7},{9,8},{10,9},{11,1... | collective-permute-start | bytes 776 | tf_op jit(solution)/shard_map/ppermute | solution.py:29
  169.8 7.4 %collective-permute-start.25 = (f32[2,32,1]{2,1,0:T(8,128)S(1)}, f32[2,32,1]{2,1,0:T(8,128)S(1)}, u32[]{:S(2)}, u32[]{:S(2)}) collective-permute-start(f32[2,32,1]{2,1,0:T(8,128)S(1)} %get-tuple-element.302), channel_id=1, source_target_pairs={{0,1},{1,2},{2,3},{3,4},{4,5},{5,6},{6,7},{7,8},{8,9},{9,10},{10,1... | collective-permute-start | bytes 776 | tf_op jit(solution)/shard_map/ppermute | solution.py:26
  178.2 16.0 %all-to-all-start.6 = ((f32[16,1,2,1,130]{4,3,2,1,0:T(1,128)}), f32[16,1,2,1,130]{4,3,2,1,0:T(1,128)S(1)}, u32[]{:S(2)}, u32[]{:S(2)}) async-start(f32[16,1,2,1,130]{4,3,2,1,0:T(1,128)} %stack.85), calls=%async_computation.6 | async-start | bytes 65536 | tf_op jit(solution)/shard_map/all_to_all | solution.py:41
  186.3 7.9 %collective-permute-start.26 = (f32[2,1,130]{2,1,0:T(1,128)S(1)}, f32[2,1,130]{2,1,0:T(1,128)S(1)}, u32[]{:S(2)}, u32[]{:S(2)}) collective-permute-start(f32[2,1,130]{2,1,0:T(1,128)S(1)} %get-tuple-element.286), channel_id=1, source_target_pairs={{16,0},{32,16},{48,32},{64,48},{80,64},{96,80},{112,96},{17,1},{33... | collective-permute-start | bytes 3128 | tf_op jit(solution)/shard_map/ppermute | solution.py:29
  187.7 7.1 %collective-permute-start.27 = (f32[2,1,130]{2,1,0:T(1,128)S(1)}, f32[2,1,130]{2,1,0:T(1,128)S(1)}, u32[]{:S(2)}, u32[]{:S(2)}) collective-permute-start(f32[2,1,130]{2,1,0:T(1,128)S(1)} %get-tuple-element.287), channel_id=1, source_target_pairs={{0,16},{16,32},{32,48},{48,64},{64,80},{80,96},{96,112},{1,17},{17... | collective-permute-start | bytes 3128 | tf_op jit(solution)/shard_map/ppermute | solution.py:26
  194.9 24.7 %copy-start.1 = (f32[32,128]{1,0:T(8,128)}, f32[32,128]{1,0:T(8,128)S(1)}, u32[]{:S(2)}) copy-start(f32[32,128]{1,0:T(8,128)S(1)} %fusion.40) | copy-start | bytes 49156
  195.0 4.9 %collective-permute-start.28 = (f32[1,32,1]{2,1,0:T(8,128)S(1)}, f32[1,32,1]{2,1,0:T(8,128)S(1)}, u32[]{:S(2)}, u32[]{:S(2)}) collective-permute-start(f32[1,32,1]{2,1,0:T(8,128)S(1)} %get-tuple-element.310), channel_id=1, source_target_pairs={{0,1},{1,2},{2,3},{3,4},{4,5},{5,6},{6,7},{7,8},{8,9},{9,10},{10,1... | collective-permute-start | bytes 392 | tf_op jit(solution)/shard_map/ppermute | solution.py:26
  199.0 4.7 collective-permute-start.29
  204.7 13.2 %all-to-all-start.7 = ((f32[16,1,1,1,130]{4,3,2,1,0:T(1,128)}), f32[16,1,1,1,130]{4,3,2,1,0:T(1,128)S(1)}, u32[]{:S(2)}, u32[]{:S(2)}) async-start(f32[16,1,1,1,130]{4,3,2,1,0:T(1,128)} %stack.86), calls=%async_computation.7 | async-start | bytes 32768 | tf_op jit(solution)/shard_map/all_to_all | solution.py:41
  210.6 5.9 %collective-permute-start.31 = (f32[1,1,130]{2,1,0:T(1,128)S(1)}, f32[1,1,130]{2,1,0:T(1,128)S(1)}, u32[]{:S(2)}, u32[]{:S(2)}) collective-permute-start(f32[1,1,130]{2,1,0:T(1,128)S(1)} %get-tuple-element.295), channel_id=1, source_target_pairs={{16,0},{32,16},{48,32},{64,48},{80,64},{96,80},{112,96},{17,1},{33... | collective-permute-start | bytes 1568 | tf_op jit(solution)/shard_map/ppermute | solution.py:29
  212.0 5.9 %collective-permute-start.30 = (f32[1,1,130]{2,1,0:T(1,128)S(1)}, f32[1,1,130]{2,1,0:T(1,128)S(1)}, u32[]{:S(2)}, u32[]{:S(2)}) collective-permute-start(f32[1,1,130]{2,1,0:T(1,128)S(1)} %get-tuple-element.294), channel_id=1, source_target_pairs={{0,16},{16,32},{32,48},{48,64},{64,80},{80,96},{96,112},{1,17},{17... | collective-permute-start | bytes 1568 | tf_op jit(solution)/shard_map/ppermute | solution.py:26
  218.1 1.6 copy-start.4
  218.1 1.6 copy-start.5
  219.7 78.1 %copy-start.2 = (f32[1,128,1024]{2,1,0:T(8,128)S(1)}, f32[1,128,1024]{2,1,0:T(8,128)}, u32[]{:S(2)}) copy-start(f32[1,128,1024]{2,1,0:T(8,128)} %param.25) | copy-start | bytes 1572868
  301.8 49.2 %all-to-all-start.9 = ((f32[4,128,1024]{2,0,1:T(4,128)}), f32[4,128,1024]{2,0,1:T(4,128)S(1)}, u32[]{:S(2)}, u32[]{:S(2)}) async-start(f32[4,128,1024]{2,0,1:T(4,128)} %copy.50), calls=%async_computation.9 | async-start | bytes 4194304 | tf_op jit(solution)/shard_map/all_to_all | solution.py:182
